TPU v7x, 512 devices: a whole 4x8x8 slice. The times are simulated.
512 devices in a mesh: wide: 32 (over z, x), tensor: 16 (over y, core).
Axes of the slice: x: 4, y: 8, z: 8, core: 2. Of those that a mesh axis runs over, the one named last changes fastest.
Arguments:
- tokens: bfloat16 [16384, 8192], P('wide', 'tensor'), may hold values from -6 to 6
- key_value_weight: bfloat16 [8192, 2048], P(None, 'tensor'), may hold values from -0.0625 to 0.0625
- adapter_down_maps: bfloat16 [8192, 512, 64], P('tensor', 'wide'), may hold values from -0.0625 to 0.0625
- adapter_up_maps: bfloat16 [512, 64, 2048], P('wide', None, 'tensor'), may hold values from -0.75 to 0.75
- adapter_per_row: int32 [16384], P('wide'), may hold values from 0 to 511, as said below
- adapter_storage_slot: int32 [512], replicated, may hold values from 0 to 511, as said below
Outputs:
- kv_out: bfloat16 [16384, 2048], P('wide', 'tensor')
Inputs may be any that keep to these rules, and one draw needn't show every extreme that they name: `adapter_per_row`: the adapter stored at position p belongs to owner p // 16 of wide. Among the 512 rows of one index of wide, at most 32 name adapters of one owner; in every draw one owner gets exactly 32 rows from every index of wide. `adapter_storage_slot`: each position is taken by exactly one adapter.
All inputs are finite; a program needn't handle non-finite values.
Results may differ from a plain program's by a relative error of at most 0.0049.
Values may be sent and summed in bfloat16 or wider, within the bound.
No kernel may reach another device: no remote copies, remote signals or barrier semaphores. Data moves between devices by JAX's collectives and lax.ppermute only.
A program may use at most 64 MiB of HBM per device.

v0:
```python
import jax
import jax.numpy as jnp
from jax import lax
from jax.sharding import PartitionSpec as P


def body(
    tokens,
    key_value_weight,
    adapter_down_maps,
    adapter_up_maps,
    adapter_per_row,
    adapter_storage_slot,
):
    row_count, feature_portion = tokens.shape
    wide_count = lax.axis_size("wide")
    tensor_count = lax.axis_size("tensor")
    capacity = 2 * row_count // wide_count
    present_adapters = adapter_down_maps.shape[1]
    rank_dimension = adapter_down_maps.shape[2]
    column_portion = key_value_weight.shape[1]
    total_adapters = adapter_storage_slot.shape[0]
    slot_count = wide_count * capacity
    lane = 128
    info_rows = 8
    gathered = lax.all_gather(tokens, "tensor", axis=1, tiled=True)
    base_projection_output = jnp.dot(gathered, key_value_weight, preferred_element_type=jnp.float32)
    adapter_match = (
        adapter_per_row[:, None] == jnp.arange(total_adapters, dtype=jnp.int32)[None, :]
    ).astype(jnp.bfloat16)
    slot_parts = jnp.stack(
        [adapter_storage_slot // present_adapters, adapter_storage_slot % present_adapters], axis=1
    ).astype(jnp.bfloat16)
    picked = jnp.dot(adapter_match, slot_parts, preferred_element_type=jnp.float32)
    owner_index = picked[:, 0].astype(jnp.int32)
    local_index = picked[:, 1].astype(jnp.int32)
    owner_onehot = (
        owner_index[:, None] == jnp.arange(wide_count, dtype=jnp.int32)[None, :]
    ).astype(jnp.float32)
    row_iota = jnp.arange(row_count, dtype=jnp.int32)
    strictly_before = (row_iota[:, None] > row_iota[None, :]).astype(jnp.float32)
    earlier = jnp.dot(strictly_before, owner_onehot, preferred_element_type=jnp.float32)
    rank_in_owner = jnp.sum(earlier * owner_onehot, axis=1).astype(jnp.int32)
    destination = owner_index * capacity + rank_in_owner
    placement = (jnp.arange(slot_count, dtype=jnp.int32)[:, None] == destination[None, :]).astype(
        jnp.bfloat16
    )
    lane_tiles = feature_portion // lane
    local_code = jnp.broadcast_to(
        (local_index + 1).astype(jnp.bfloat16)[:, None], (row_count, lane)
    )
    placement_blocks = placement.reshape(wide_count, capacity, row_count)
    token_tiles = tokens.reshape(row_count, lane_tiles, lane)
    placed = jnp.einsum(
        "dcr,rjl->djcl", placement_blocks, token_tiles, preferred_element_type=jnp.float32
    ).astype(jnp.bfloat16)
    pieces = [placed.reshape(wide_count, lane_tiles * capacity, lane)]
    placed_code = jnp.dot(placement, local_code, preferred_element_type=jnp.float32)
    slot_code = placed_code[:, 0].astype(jnp.bfloat16).reshape(wide_count, 1, capacity)
    pieces.append(jnp.pad(slot_code, ((0, 0), (0, info_rows - 1), (0, lane - capacity))))
    send_block = jnp.concatenate(pieces, axis=1)
    got_block = lax.all_to_all(send_block, "wide", split_axis=0, concat_axis=0, tiled=True)
    flat_rows = jnp.concatenate(
        [
            got_block[:, tile * capacity : (tile + 1) * capacity, :].reshape(slot_count, lane)
            for tile in range(lane_tiles)
        ],
        axis=1,
    )
    got_code = got_block[:, lane_tiles * capacity, :capacity].reshape(slot_count).astype(jnp.int32)
    selected = (got_code[:, None] == jnp.arange(1, present_adapters + 1, dtype=jnp.int32)[None, :])[
        :, :, None
    ]
    down_matrix = adapter_down_maps.reshape(feature_portion, present_adapters * rank_dimension)
    all_ranks = jnp.dot(flat_rows, down_matrix, preferred_element_type=jnp.float32)
    all_ranks = all_ranks.reshape(slot_count, present_adapters, rank_dimension)
    partial_value = jnp.sum(jnp.where(selected, all_ranks, 0.0), axis=1)
    block_rows = slot_count // tensor_count
    dense_shape = (tensor_count, block_rows * rank_dimension // 128, 128)
    slot_blocks = partial_value.reshape(dense_shape)
    gathered_blocks = lax.all_to_all(slot_blocks, "tensor", split_axis=0, concat_axis=0, tiled=True)
    own_sum = jnp.sum(gathered_blocks, axis=0).astype(jnp.bfloat16)
    spread_shape = (tensor_count, 16, block_rows * rank_dimension // 16)
    spread = jnp.broadcast_to(own_sum.reshape(spread_shape[1:])[None], spread_shape)
    reduced_rows = lax.all_to_all(spread, "tensor", split_axis=0, concat_axis=0, tiled=True)
    reduced_rows = reduced_rows.reshape(slot_count, rank_dimension)
    base_tie = (base_projection_output[0, 0] * 0.0).astype(jnp.bfloat16)
    expanded_rows = jnp.where(
        selected, reduced_rows[:, None, :] + base_tie, jnp.zeros((), jnp.bfloat16)
    ).reshape(slot_count, present_adapters * rank_dimension)
    up_matrix = adapter_up_maps.reshape(present_adapters * rank_dimension, column_portion)
    adapter_correction = jnp.dot(
        expanded_rows, up_matrix, preferred_element_type=jnp.float32
    ).astype(jnp.bfloat16)
    adapter_correction = adapter_correction.reshape(wide_count, capacity, column_portion)
    returned_rows = lax.all_to_all(
        adapter_correction, "wide", split_axis=0, concat_axis=0, tiled=True
    )
    returned_rows = returned_rows.reshape(slot_count, column_portion)
    adapter_row_output = jnp.dot(placement.T, returned_rows, preferred_element_type=jnp.float32)
    return (base_projection_output + adapter_row_output).astype(jnp.bfloat16)


def solution(mesh):
    in_specs = (
        P("wide", "tensor"),
        P(None, "tensor"),
        P("tensor", "wide", None),
        P("wide", None, "tensor"),
        P("wide"),
        P(),
    )
    out_specs = P("wide", "tensor")
    return jax.shard_map(body, mesh=mesh, in_specs=in_specs, out_specs=out_specs, check_vma=False)
```

profile of v0, /device:TPU:1, one launch (start us, length us, event | category | flops | bytes accessed | tf_op | source)
XLA Modules:
  0.0 120.1 jit_solution(7140281131898327111)
XLA Ops:
  6.5 0.7 all-gather.2.cloned.1.call-update
  7.3 0.8 fusion.42
  8.0 1.1 fusion.35
  9.1 0.3 fusion.20
  9.4 0.6 fusion.4
  10.2 0.8 fusion.9
  10.9 1.2 fusion.21
  12.1 13.7 %all-to-all-start = ((bf16[32,136,128]{2,1,0:T(8,128)(2,1)}), bf16[32,136,128]{2,1,0:T(8,128)(2,1)S(1)}, u32[]{:S(2)}, u32[]{:S(2)}) async-start(bf16[32,136,128]{2,1,0:T(8,128)(2,1)} %fusion.21), calls=%async_computation | async-start | bytes 2228224 | tf_op jit(solution)/shard_map/all_to_all | solution.py:62
  25.8 27.3 %all-to-all-done = bf16[32,136,128]{2,1,0:T(8,128)(2,1)S(1)} async-done(((bf16[32,136,128]{2,1,0:T(8,128)(2,1)}), bf16[32,136,128]{2,1,0:T(8,128)(2,1)S(1)}, u32[]{:S(2)}, u32[]{:S(2)}) %all-to-all-start) | async-done | bytes 1114144 | tf_op jit(solution)/shard_map/all_to_all | solution.py:62
  53.5 1.0 copy-done.2
  54.5 1.3 %select_reduce_fusion = f32[1024,64]{0,1:T(8,128)S(1)} fusion(pred[1024,16]{0,1:T(8,128)(4,1)S(1)} %broadcast_compare_fusion, bf16[1024,128]{1,0:T(8,128)(2,1)S(1)} %bitcast.51, bf16[1024,128]{1,0:T(8,128)(2,1)S(1)} %bitcast.52, bf16[1024,128]{1,0:T(8,128)(2,1)S(1)} %bitcast.53, bf16[1024,128]{1,0:T(8,128)(2,1)S(1)} %bitcast.50, ...), kind=kOutput, calls=%fused_computation | convolution fusion | flops 1079967744 | bytes 2375680 | tf_op jit(solution)/shard_map/dot_general | solution.py:75
  55.8 0.2 copy.14
  56.0 0.1 reshape.141
  56.2 23.4 %all_to_all.20 = f32[16,32,128]{2,1,0:T(8,128)S(1)} all-to-all(f32[16,32,128]{2,1,0:T(8,128)S(1)} %reshape.141), channel_id=1, replica_groups=mesh['wide'=32,'tensor'=16] {'tensor'}, dimensions={0} | all-to-all | bytes 524288 | tf_op jit(solution)/shard_map/all_to_all | solution.py:81
  79.6 0.7 broadcast_in_dim.58
  80.2 3.4 %all-to-all-start.2 = ((bf16[16,16,256]{2,1,0:T(8,128)(2,1)}), bf16[16,16,256]{2,1,0:T(8,128)(2,1)S(1)}, u32[]{:S(2)}, u32[]{:S(2)}) async-start(bf16[16,16,256]{2,1,0:T(8,128)(2,1)} %broadcast_in_dim.58), calls=%async_computation.2 | async-start | bytes 262144 | tf_op jit(solution)/shard_map/all_to_all | solution.py:85
  83.7 5.7 %fusion.55 = f32[512,128]{1,0:T(8,128)S(1)} fusion(bf16[512,8192]{1,0:T(8,128)(2,1)} %all-gather.2.cloned.1.call-done, bf16[8192,128]{1,0:T(8,128)(2,1)S(1)} %copy-done), kind=kOutput, calls=%fused_computation.75 | convolution fusion | flops 1073741824 | bytes 10747904 | tf_op jit(solution)/shard_map/dot_general | solution.py:27
  89.5 0.6 slice.45
  90.8 1.4 %all-to-all-done.2 = bf16[16,16,256]{2,1,0:T(8,128)(2,1)S(1)} async-done(((bf16[16,16,256]{2,1,0:T(8,128)(2,1)}), bf16[16,16,256]{2,1,0:T(8,128)(2,1)S(1)}, u32[]{:S(2)}, u32[]{:S(2)}) %all-to-all-start.2) | async-done | bytes 131104 | tf_op jit(solution)/shard_map/all_to_all | solution.py:85
  92.1 0.2 add.55
  92.3 0.1 copy.15
  92.5 0.8 fusion.15
  93.2 18.7 %all_to_all.21 = bf16[32,32,128]{2,1,0:T(8,128)(2,1)S(1)} all-to-all(bf16[32,32,128]{2,1,0:T(8,128)(2,1)S(1)} %bitcast.49), channel_id=1, replica_groups=mesh['wide'=32,'tensor'=16] {'wide'}, dimensions={0} | all-to-all | bytes 524288 | tf_op jit(solution)/shard_map/all_to_all | solution.py:96
  111.9 1.4 %fusion.19 = bf16[512,128]{1,0:T(8,128)(2,1)} fusion(f32[512,128]{1,0:T(8,128)S(1)} %fusion.55, bf16[1024,128]{1,0:T(8,128)(2,1)S(1)} %bitcast.48, s32[512]{0:T(512)S(1)} %convert_add_fusion), kind=kOutput, calls=%fused_computation.16 | convolution fusion | flops 134873088 | bytes 657408 | tf_op jit(solution)/shard_map/dot_general | solution.py:100
  (26 shorter events, 0.6 us)
Async XLA Ops:
  6.5 77.2 %copy-start = (bf16[8192,128]{1,0:T(8,128)(2,1)S(1)}, bf16[8192,128]{1,0:T(8,128)(2,1)}, u32[]{:S(2)}) copy-start(bf16[8192,128]{1,0:T(8,128)(2,1)} %param.7) | copy-start | bytes 6291460
  6.5 3.6 %copy-start.1 = (bf16[512,512]{1,0:T(8,128)(2,1)S(1)}, bf16[512,512]{1,0:T(8,128)(2,1)}, u32[]{:S(2)}) copy-start(bf16[512,512]{1,0:T(8,128)(2,1)} %param.6) | copy-start | bytes 1572868
  6.5 77.2 %all-gather.2.cloned.1.call-start = ((), (), s32[]{:S(2)}) async-start(), calls=%async_computation.4 | async-start | bytes 8912896 | tf_op jit(solution)/shard_map/all_gather | solution.py:26
  12.1 41.1 %all-to-all-start = ((bf16[32,136,128]{2,1,0:T(8,128)(2,1)}), bf16[32,136,128]{2,1,0:T(8,128)(2,1)S(1)}, u32[]{:S(2)}, u32[]{:S(2)}) async-start(bf16[32,136,128]{2,1,0:T(8,128)(2,1)} %fusion.21), calls=%async_computation | async-start | bytes 2228224 | tf_op jit(solution)/shard_map/all_to_all | solution.py:62
  53.3 1.2 %copy-start.2 = (bf16[512,16,64]{0,2,1:T(8,128)(2,1)S(1)}, bf16[512,16,64]{0,2,1:T(8,128)(2,1)}, u32[]{:S(2)}) copy-start(bf16[512,16,64]{0,2,1:T(8,128)(2,1)} %param.8) | copy-start | bytes 3145732
  80.2 11.9 %all-to-all-start.2 = ((bf16[16,16,256]{2,1,0:T(8,128)(2,1)}), bf16[16,16,256]{2,1,0:T(8,128)(2,1)S(1)}, u32[]{:S(2)}, u32[]{:S(2)}) async-start(bf16[16,16,256]{2,1,0:T(8,128)(2,1)} %broadcast_in_dim.58), calls=%async_computation.2 | async-start | bytes 262144 | tf_op jit(solution)/shard_map/all_to_all | solution.py:85
  83.7 8.8 %copy-start.3 = (bf16[16,64,128]{2,1,0:T(8,128)(2,1)S(1)}, bf16[16,64,128]{2,1,0:T(8,128)(2,1)}, u32[]{:S(2)}) copy-start(bf16[16,64,128]{2,1,0:T(8,128)(2,1)} %param.9) | copy-start | bytes 786436
Sparse Core Ops, SparseCore 0:
  9.5 67.3 all-gather.1
where the time goes:
time: 121 us; the launch traced here: 120 us
  blocking collectives  42 us (35%)
  waiting for transfers between devices  29.4 us (24%)
  starting transfers between devices  17.1 us (14%)
  between operations  14.3 us (12%)
  matrix products  11.9 us (10%)
  local copies, waits for them, and re-layouts  3.23 us (3%)
  other arithmetic  2.17 us (2%)
    all_to_all x1, waiting for transfers between devices, body(): lax.all_to_all(send_block, 'wide', split_axis=0, concat_axis=0, tiled=True)  27.3 us
    all_to_all x1, blocking collectives, body(): lax.all_to_all(slot_blocks, 'tensor', split_axis=0, concat_axis=0, tiled=...  23.4 us
    all_to_all x1, blocking collectives, body(): lax.all_to_all(adapter_correction, 'wide', split_axis=0, concat_axis=0, t...  18.7 us
    all_to_all x1, starting transfers between devices, body(): lax.all_to_all(send_block, 'wide', split_axis=0, concat_axis=0, tiled=True)  13.7 us
    dot_general x1, matrix products, body(): jnp.dot(gathered, key_value_weight, preferred_element_type=jnp.float32)  5.74 us
    all_to_all x1, starting transfers between devices, body(): lax.all_to_all(spread, 'tensor', split_axis=0, concat_axis=0, tiled=True)  3.41 us
  transfers between devices with their start and end apart: 3, of which 2 were waited for; matrix products, arithmetic and copies ran while one was open for 11% of the time, Pallas kernels for 0%

commit v1 on v0

--- a/solution.py
+++ b/solution.py
@@ -2,6 +2,28 @@
 import jax.numpy as jnp
 from jax import lax
 from jax.sharding import PartitionSpec as P
+
+
+def cut_along(value, dim, length):
+    before, after = (value.shape[:dim], value.shape[dim + 1 :])
+    return jnp.moveaxis(value.reshape(*before, length, -1, *after), dim, 0)
+
+
+def joined_along(blocks, dim):
+    blocks = jnp.moveaxis(blocks, 0, dim)
+    shape = blocks.shape
+    return blocks.reshape(*shape[:dim], shape[dim] * shape[dim + 1], *shape[dim + 2 :])
+
+
+def exchange_in_pairs(x, axis, split_dim, concat_dim):
+    peers, index = (lax.axis_size(axis), lax.axis_index(axis))
+    blocks = cut_along(x, split_dim, peers)
+    outs = [blocks[index]]
+    for step in range(1, peers):
+        sent = blocks[index ^ step]
+        outs.append(lax.ppermute(sent, axis, [(i, i ^ step) for i in range(peers)]))
+    blocks = jnp.stack(outs)[index ^ jnp.arange(peers)]
+    return joined_along(blocks, concat_dim)
 
 
 def body(
@@ -82,7 +104,7 @@
     own_sum = jnp.sum(gathered_blocks, axis=0).astype(jnp.bfloat16)
     spread_shape = (tensor_count, 16, block_rows * rank_dimension // 16)
     spread = jnp.broadcast_to(own_sum.reshape(spread_shape[1:])[None], spread_shape)
-    reduced_rows = lax.all_to_all(spread, "tensor", split_axis=0, concat_axis=0, tiled=True)
+    reduced_rows = exchange_in_pairs(spread, "tensor", 0, 0)
     reduced_rows = reduced_rows.reshape(slot_count, rank_dimension)
     base_tie = (base_projection_output[0, 0] * 0.0).astype(jnp.bfloat16)
     expanded_rows = jnp.where(

time: 121 us -> 175 us (1.45); the launches traced: 120 us -> 171 us
  starting transfers between devices: 17.1 us -> 78.1 us
  blocking collectives: 42 us -> 19.1 us
  waiting for transfers between devices: 29.4 us -> 41.8 us
    ppermute x0 -> x15, starting transfers between devices: none -> 54.2 us  [exchange_in_pairs(): outs.append(lax.ppermute(sent, axis, [(i, i ^ step) for i in range(peers)]))]
    all_to_all x1 -> x0, blocking collectives: 23.4 us -> none  [body(): lax.all_to_all(slot_blocks, 'tensor', split_axis=0, concat_axis=0, tiled=...]
    all_to_all x1, waiting for transfers between devices: 1.37 us -> 12.4 us  [body(): lax.all_to_all(slot_blocks, 'tensor', split_axis=0, concat_axis=0, tiled=...]
    all_to_all x1, starting transfers between devices: 3.41 us -> 10.2 us  [body(): lax.all_to_all(slot_blocks, 'tensor', split_axis=0, concat_axis=0, tiled=...]
  transfers between devices with their start and end apart: 3 -> 18, of which waited for: 2 -> 3; matrix products, arithmetic and copies ran while one was open for 11% -> 5% of each run, Pallas kernels for 0% -> 0%
where the time goes in v1:
time: 175 us; the launch traced here: 171 us
  starting transfers between devices  78.1 us (45%)
  waiting for transfers between devices  41.8 us (24%)
  blocking collectives  19.1 us (11%)
  between operations  14.6 us (8%)
  matrix products  11.9 us (7%)
  local copies, waits for them, and re-layouts  3.85 us (2%)
  other arithmetic  2.19 us (1%)
    ppermute x15, starting transfers between devices, exchange_in_pairs(): outs.append(lax.ppermute(sent, axis, [(i, i ^ step) for i in range(peers)]))  54.2 us
    all_to_all x1, waiting for transfers between devices, body(): lax.all_to_all(send_block, 'wide', split_axis=0, concat_axis=0, tiled=True)  27.3 us
    all_to_all x1, blocking collectives, body(): lax.all_to_all(adapter_correction, 'wide', split_axis=0, concat_axis=0, t...  19.1 us
    all_to_all x1, starting transfers between devices, body(): lax.all_to_all(send_block, 'wide', split_axis=0, concat_axis=0, tiled=True)  13.7 us
    all_to_all x1, waiting for transfers between devices, body(): lax.all_to_all(slot_blocks, 'tensor', split_axis=0, concat_axis=0, tiled=...  12.4 us
    all_to_all x1, starting transfers between devices, body(): lax.all_to_all(slot_blocks, 'tensor', split_axis=0, concat_axis=0, tiled=...  10.2 us
    dot_general x1, matrix products, body(): jnp.dot(gathered, key_value_weight, preferred_element_type=jnp.float32)  5.74 us
  transfers between devices with their start and end apart: 18, of which 3 were waited for; matrix products, arithmetic and copies ran while one was open for 5% of the time, Pallas kernels for 0%

profile of v1, /device:TPU:1, one launch (start us, length us, event | category | flops | bytes accessed | tf_op | source)
XLA Modules:
  0.0 171.4 jit_solution(8080477796267139494)
XLA Ops:
  12.1 13.7 %all-to-all-start = ((bf16[32,136,128]{2,1,0:T(8,128)(2,1)}), bf16[32,136,128]{2,1,0:T(8,128)(2,1)S(1)}, u32[]{:S(2)}, u32[]{:S(2)}) async-start(bf16[32,136,128]{2,1,0:T(8,128)(2,1)} %fusion.21), calls=%async_computation | async-start | bytes 2228224 | tf_op jit(solution)/shard_map/all_to_all | solution.py:84
  25.8 27.3 %all-to-all-done = bf16[32,136,128]{2,1,0:T(8,128)(2,1)S(1)} async-done(((bf16[32,136,128]{2,1,0:T(8,128)(2,1)}), bf16[32,136,128]{2,1,0:T(8,128)(2,1)S(1)}, u32[]{:S(2)}, u32[]{:S(2)}) %all-to-all-start) | async-done | bytes 1114144 | tf_op jit(solution)/shard_map/all_to_all | solution.py:84
  54.5 1.3 select_reduce_fusion
  56.9 10.2 %all-to-all-start.1 = ((f32[16,32,128]{2,1,0:T(8,128)}), f32[16,32,128]{2,1,0:T(8,128)S(1)}, u32[]{:S(2)}, u32[]{:S(2)}) async-start(f32[16,32,128]{2,1,0:T(8,128)} %reshape.203), calls=%async_computation.1 | async-start | bytes 524288 | tf_op jit(solution)/shard_map/all_to_all | solution.py:103
  67.1 12.4 %all-to-all-done.1 = f32[16,32,128]{2,1,0:T(8,128)S(1)} async-done(((f32[16,32,128]{2,1,0:T(8,128)}), f32[16,32,128]{2,1,0:T(8,128)S(1)}, u32[]{:S(2)}, u32[]{:S(2)}) %all-to-all-start.1) | async-done | bytes 262176 | tf_op jit(solution)/shard_map/all_to_all | solution.py:103
  79.6 1.9 %collective-permute-start = (bf16[1,16,256]{2,1,0:T(8,128)(2,1)S(1)}, bf16[1,16,256]{2,1,0:T(8,128)(2,1)S(1)}, u32[]{:S(2)}, u32[]{:S(2)}) collective-permute-start(bf16[1,16,256]{2,1,0:T(8,128)(2,1)S(1)} %convert_element_type.102), channel_id=1, source_target_pairs={{0,1},{1,0},{2,3},{3,2},{4,5},{5,4},{6,7},{7,6},{8,9},{9,8},{10,11... | collective-permute-start | bytes 24584 | tf_op jit(solution)/shard_map/ppermute | solution.py:24
  81.5 1.9 %collective-permute-start.1 = (bf16[1,16,256]{2,1,0:T(8,128)(2,1)S(1)}, bf16[1,16,256]{2,1,0:T(8,128)(2,1)S(1)}, u32[]{:S(2)}, u32[]{:S(2)}) collective-permute-start(bf16[1,16,256]{2,1,0:T(8,128)(2,1)S(1)} %convert_element_type.102), channel_id=1, source_target_pairs={{0,2},{1,3},{2,0},{3,1},{4,6},{5,7},{6,4},{7,5},{8,10},{9,11},{10,... | collective-permute-start | bytes 24584 | tf_op jit(solution)/shard_map/ppermute | solution.py:24
  83.5 4.0 %collective-permute-start.2 = (bf16[1,16,256]{2,1,0:T(8,128)(2,1)S(1)}, bf16[1,16,256]{2,1,0:T(8,128)(2,1)S(1)}, u32[]{:S(2)}, u32[]{:S(2)}) collective-permute-start(bf16[1,16,256]{2,1,0:T(8,128)(2,1)S(1)} %convert_element_type.102), channel_id=1, source_target_pairs={{0,3},{1,2},{2,1},{3,0},{4,7},{5,6},{6,5},{7,4},{8,11},{9,10},{10,... | collective-permute-start | bytes 24584 | tf_op jit(solution)/shard_map/ppermute | solution.py:24
  87.5 2.2 %collective-permute-start.3 = (bf16[1,16,256]{2,1,0:T(8,128)(2,1)S(1)}, bf16[1,16,256]{2,1,0:T(8,128)(2,1)S(1)}, u32[]{:S(2)}, u32[]{:S(2)}) collective-permute-start(bf16[1,16,256]{2,1,0:T(8,128)(2,1)S(1)} %convert_element_type.102), channel_id=1, source_target_pairs={{0,4},{1,5},{2,6},{3,7},{4,0},{5,1},{6,2},{7,3},{8,12},{9,13},{10,... | collective-permute-start | bytes 24584 | tf_op jit(solution)/shard_map/ppermute | solution.py:24
  89.7 3.9 %collective-permute-start.4 = (bf16[1,16,256]{2,1,0:T(8,128)(2,1)S(1)}, bf16[1,16,256]{2,1,0:T(8,128)(2,1)S(1)}, u32[]{:S(2)}, u32[]{:S(2)}) collective-permute-start(bf16[1,16,256]{2,1,0:T(8,128)(2,1)S(1)} %convert_element_type.102), channel_id=1, source_target_pairs={{0,5},{1,4},{2,7},{3,6},{4,1},{5,0},{6,3},{7,2},{8,13},{9,12},{10,... | collective-permute-start | bytes 24584 | tf_op jit(solution)/shard_map/ppermute | solution.py:24
  93.6 3.0 %collective-permute-start.5 = (bf16[1,16,256]{2,1,0:T(8,128)(2,1)S(1)}, bf16[1,16,256]{2,1,0:T(8,128)(2,1)S(1)}, u32[]{:S(2)}, u32[]{:S(2)}) collective-permute-start(bf16[1,16,256]{2,1,0:T(8,128)(2,1)S(1)} %convert_element_type.102), channel_id=1, source_target_pairs={{0,6},{1,7},{2,4},{3,5},{4,2},{5,3},{6,0},{7,1},{8,14},{9,15},{10,... | collective-permute-start | bytes 24584 | tf_op jit(solution)/shard_map/ppermute | solution.py:24
  96.6 4.7 %collective-permute-start.6 = (bf16[1,16,256]{2,1,0:T(8,128)(2,1)S(1)}, bf16[1,16,256]{2,1,0:T(8,128)(2,1)S(1)}, u32[]{:S(2)}, u32[]{:S(2)}) collective-permute-start(bf16[1,16,256]{2,1,0:T(8,128)(2,1)S(1)} %convert_element_type.102), channel_id=1, source_target_pairs={{0,7},{1,6},{2,5},{3,4},{4,3},{5,2},{6,1},{7,0},{8,15},{9,14},{10,... | collective-permute-start | bytes 24584 | tf_op jit(solution)/shard_map/ppermute | solution.py:24
  101.4 2.7 %collective-permute-start.7 = (bf16[1,16,256]{2,1,0:T(8,128)(2,1)S(1)}, bf16[1,16,256]{2,1,0:T(8,128)(2,1)S(1)}, u32[]{:S(2)}, u32[]{:S(2)}) collective-permute-start(bf16[1,16,256]{2,1,0:T(8,128)(2,1)S(1)} %convert_element_type.102), channel_id=1, source_target_pairs={{0,8},{1,9},{2,10},{3,11},{4,12},{5,13},{6,14},{7,15},{8,0},{9,1},... | collective-permute-start | bytes 24584 | tf_op jit(solution)/shard_map/ppermute | solution.py:24
  104.2 6.4 %collective-permute-start.8 = (bf16[1,16,256]{2,1,0:T(8,128)(2,1)S(1)}, bf16[1,16,256]{2,1,0:T(8,128)(2,1)S(1)}, u32[]{:S(2)}, u32[]{:S(2)}) collective-permute-start(bf16[1,16,256]{2,1,0:T(8,128)(2,1)S(1)} %convert_element_type.102), channel_id=1, source_target_pairs={{0,9},{1,8},{2,11},{3,10},{4,13},{5,12},{6,15},{7,14},{8,1},{9,0},... | collective-permute-start | bytes 24584 | tf_op jit(solution)/shard_map/ppermute | solution.py:24
  110.6 1.9 %collective-permute-start.9 = (bf16[1,16,256]{2,1,0:T(8,128)(2,1)S(1)}, bf16[1,16,256]{2,1,0:T(8,128)(2,1)S(1)}, u32[]{:S(2)}, u32[]{:S(2)}) collective-permute-start(bf16[1,16,256]{2,1,0:T(8,128)(2,1)S(1)} %convert_element_type.102), channel_id=1, source_target_pairs={{0,10},{1,11},{2,8},{3,9},{4,14},{5,15},{6,12},{7,13},{8,2},{9,3},... | collective-permute-start | bytes 24584 | tf_op jit(solution)/shard_map/ppermute | solution.py:24
  112.5 7.0 %collective-permute-start.10 = (bf16[1,16,256]{2,1,0:T(8,128)(2,1)S(1)}, bf16[1,16,256]{2,1,0:T(8,128)(2,1)S(1)}, u32[]{:S(2)}, u32[]{:S(2)}) collective-permute-start(bf16[1,16,256]{2,1,0:T(8,128)(2,1)S(1)} %convert_element_type.102), channel_id=1, source_target_pairs={{0,11},{1,10},{2,9},{3,8},{4,15},{5,14},{6,13},{7,12},{8,3},{9,2},... | collective-permute-start | bytes 24584 | tf_op jit(solution)/shard_map/ppermute | solution.py:24
  119.6 1.9 %collective-permute-start.11 = (bf16[1,16,256]{2,1,0:T(8,128)(2,1)S(1)}, bf16[1,16,256]{2,1,0:T(8,128)(2,1)S(1)}, u32[]{:S(2)}, u32[]{:S(2)}) collective-permute-start(bf16[1,16,256]{2,1,0:T(8,128)(2,1)S(1)} %convert_element_type.102), channel_id=1, source_target_pairs={{0,12},{1,13},{2,14},{3,15},{4,8},{5,9},{6,10},{7,11},{8,4},{9,5},... | collective-permute-start | bytes 24584 | tf_op jit(solution)/shard_map/ppermute | solution.py:24
  121.5 5.4 %collective-permute-start.12 = (bf16[1,16,256]{2,1,0:T(8,128)(2,1)S(1)}, bf16[1,16,256]{2,1,0:T(8,128)(2,1)S(1)}, u32[]{:S(2)}, u32[]{:S(2)}) collective-permute-start(bf16[1,16,256]{2,1,0:T(8,128)(2,1)S(1)} %convert_element_type.102), channel_id=1, source_target_pairs={{0,13},{1,12},{2,15},{3,14},{4,9},{5,8},{6,11},{7,10},{8,5},{9,4},... | collective-permute-start | bytes 24584 | tf_op jit(solution)/shard_map/ppermute | solution.py:24
  126.9 1.9 %collective-permute-start.13 = (bf16[1,16,256]{2,1,0:T(8,128)(2,1)S(1)}, bf16[1,16,256]{2,1,0:T(8,128)(2,1)S(1)}, u32[]{:S(2)}, u32[]{:S(2)}) collective-permute-start(bf16[1,16,256]{2,1,0:T(8,128)(2,1)S(1)} %convert_element_type.102), channel_id=1, source_target_pairs={{0,14},{1,15},{2,12},{3,13},{4,10},{5,11},{6,8},{7,9},{8,6},{9,7},... | collective-permute-start | bytes 24584 | tf_op jit(solution)/shard_map/ppermute | solution.py:24
  128.9 5.2 %collective-permute-start.14 = (bf16[1,16,256]{2,1,0:T(8,128)(2,1)S(1)}, bf16[1,16,256]{2,1,0:T(8,128)(2,1)S(1)}, u32[]{:S(2)}, u32[]{:S(2)}) collective-permute-start(bf16[1,16,256]{2,1,0:T(8,128)(2,1)S(1)} %convert_element_type.102), channel_id=1, source_target_pairs={{0,15},{1,14},{2,13},{3,12},{4,11},{5,10},{6,9},{7,8},{8,7},{9,6},... | collective-permute-start | bytes 24584 | tf_op jit(solution)/shard_map/ppermute | solution.py:24
  134.2 1.2 collective-permute-done.14
  136.0 5.7 %fusion.56 = f32[512,128]{1,0:T(8,128)S(1)} fusion(bf16[512,8192]{1,0:T(8,128)(2,1)} %all-gather.2.cloned.1.call-done, bf16[8192,128]{1,0:T(8,128)(2,1)S(1)} %copy-done), kind=kOutput, calls=%fused_computation.95 | convolution fusion | flops 1073741824 | bytes 10747904 | tf_op jit(solution)/shard_map/dot_general | solution.py:49
  144.1 19.1 %all_to_all.15 = bf16[32,32,128]{2,1,0:T(8,128)(2,1)S(1)} all-to-all(bf16[32,32,128]{2,1,0:T(8,128)(2,1)S(1)} %bitcast.82), channel_id=1, replica_groups=mesh['wide'=32,'tensor'=16] {'wide'}, dimensions={0} | all-to-all | bytes 524288 | tf_op jit(solution)/shard_map/all_to_all | solution.py:118
  163.1 1.4 fusion.19
  (74 shorter events, 10.3 us)
Async XLA Ops:
  6.5 129.5 %copy-start = (bf16[8192,128]{1,0:T(8,128)(2,1)S(1)}, bf16[8192,128]{1,0:T(8,128)(2,1)}, u32[]{:S(2)}) copy-start(bf16[8192,128]{1,0:T(8,128)(2,1)} %param.7) | copy-start | bytes 6291460
  6.5 3.6 %copy-start.1 = (bf16[512,512]{1,0:T(8,128)(2,1)S(1)}, bf16[512,512]{1,0:T(8,128)(2,1)}, u32[]{:S(2)}) copy-start(bf16[512,512]{1,0:T(8,128)(2,1)} %param.6) | copy-start | bytes 1572868
  6.5 129.5 %all-gather.2.cloned.1.call-start = ((), (), s32[]{:S(2)}) async-start(), calls=%async_computation.3 | async-start | bytes 8912896 | tf_op jit(solution)/shard_map/all_gather | solution.py:48
  12.1 41.1 %all-to-all-start = ((bf16[32,136,128]{2,1,0:T(8,128)(2,1)}), bf16[32,136,128]{2,1,0:T(8,128)(2,1)S(1)}, u32[]{:S(2)}, u32[]{:S(2)}) async-start(bf16[32,136,128]{2,1,0:T(8,128)(2,1)} %fusion.21), calls=%async_computation | async-start | bytes 2228224 | tf_op jit(solution)/shard_map/all_to_all | solution.py:84
  53.3 1.2 copy-start.2
  56.9 22.6 %all-to-all-start.1 = ((f32[16,32,128]{2,1,0:T(8,128)}), f32[16,32,128]{2,1,0:T(8,128)S(1)}, u32[]{:S(2)}, u32[]{:S(2)}) async-start(f32[16,32,128]{2,1,0:T(8,128)} %reshape.203), calls=%async_computation.1 | async-start | bytes 524288 | tf_op jit(solution)/shard_map/all_to_all | solution.py:103
  79.6 14.0 %collective-permute-start = (bf16[1,16,256]{2,1,0:T(8,128)(2,1)S(1)}, bf16[1,16,256]{2,1,0:T(8,128)(2,1)S(1)}, u32[]{:S(2)}, u32[]{:S(2)}) collective-permute-start(bf16[1,16,256]{2,1,0:T(8,128)(2,1)S(1)} %convert_element_type.102), channel_id=1, source_target_pairs={{0,1},{1,0},{2,3},{3,2},{4,5},{5,4},{6,7},{7,6},{8,9},{9,8},{10,11... | collective-permute-start | bytes 24584 | tf_op jit(solution)/shard_map/ppermute | solution.py:24
  81.5 15.1 %collective-permute-start.1 = (bf16[1,16,256]{2,1,0:T(8,128)(2,1)S(1)}, bf16[1,16,256]{2,1,0:T(8,128)(2,1)S(1)}, u32[]{:S(2)}, u32[]{:S(2)}) collective-permute-start(bf16[1,16,256]{2,1,0:T(8,128)(2,1)S(1)} %convert_element_type.102), channel_id=1, source_target_pairs={{0,2},{1,3},{2,0},{3,1},{4,6},{5,7},{6,4},{7,5},{8,10},{9,11},{10,... | collective-permute-start | bytes 24584 | tf_op jit(solution)/shard_map/ppermute | solution.py:24
  83.5 17.9 %collective-permute-start.2 = (bf16[1,16,256]{2,1,0:T(8,128)(2,1)S(1)}, bf16[1,16,256]{2,1,0:T(8,128)(2,1)S(1)}, u32[]{:S(2)}, u32[]{:S(2)}) collective-permute-start(bf16[1,16,256]{2,1,0:T(8,128)(2,1)S(1)} %convert_element_type.102), channel_id=1, source_target_pairs={{0,3},{1,2},{2,1},{3,0},{4,7},{5,6},{6,5},{7,4},{8,11},{9,10},{10,... | collective-permute-start | bytes 24584 | tf_op jit(solution)/shard_map/ppermute | solution.py:24
  87.5 16.7 %collective-permute-start.3 = (bf16[1,16,256]{2,1,0:T(8,128)(2,1)S(1)}, bf16[1,16,256]{2,1,0:T(8,128)(2,1)S(1)}, u32[]{:S(2)}, u32[]{:S(2)}) collective-permute-start(bf16[1,16,256]{2,1,0:T(8,128)(2,1)S(1)} %convert_element_type.102), channel_id=1, source_target_pairs={{0,4},{1,5},{2,6},{3,7},{4,0},{5,1},{6,2},{7,3},{8,12},{9,13},{10,... | collective-permute-start | bytes 24584 | tf_op jit(solution)/shard_map/ppermute | solution.py:24
  89.7 20.9 %collective-permute-start.4 = (bf16[1,16,256]{2,1,0:T(8,128)(2,1)S(1)}, bf16[1,16,256]{2,1,0:T(8,128)(2,1)S(1)}, u32[]{:S(2)}, u32[]{:S(2)}) collective-permute-start(bf16[1,16,256]{2,1,0:T(8,128)(2,1)S(1)} %convert_element_type.102), channel_id=1, source_target_pairs={{0,5},{1,4},{2,7},{3,6},{4,1},{5,0},{6,3},{7,2},{8,13},{9,12},{10,... | collective-permute-start | bytes 24584 | tf_op jit(solution)/shard_map/ppermute | solution.py:24
  93.6 18.9 %collective-permute-start.5 = (bf16[1,16,256]{2,1,0:T(8,128)(2,1)S(1)}, bf16[1,16,256]{2,1,0:T(8,128)(2,1)S(1)}, u32[]{:S(2)}, u32[]{:S(2)}) collective-permute-start(bf16[1,16,256]{2,1,0:T(8,128)(2,1)S(1)} %convert_element_type.102), channel_id=1, source_target_pairs={{0,6},{1,7},{2,4},{3,5},{4,2},{5,3},{6,0},{7,1},{8,14},{9,15},{10,... | collective-permute-start | bytes 24584 | tf_op jit(solution)/shard_map/ppermute | solution.py:24
  96.6 22.9 %collective-permute-start.6 = (bf16[1,16,256]{2,1,0:T(8,128)(2,1)S(1)}, bf16[1,16,256]{2,1,0:T(8,128)(2,1)S(1)}, u32[]{:S(2)}, u32[]{:S(2)}) collective-permute-start(bf16[1,16,256]{2,1,0:T(8,128)(2,1)S(1)} %convert_element_type.102), channel_id=1, source_target_pairs={{0,7},{1,6},{2,5},{3,4},{4,3},{5,2},{6,1},{7,0},{8,15},{9,14},{10,... | collective-permute-start | bytes 24584 | tf_op jit(solution)/shard_map/ppermute | solution.py:24
  101.4 20.1 %collective-permute-start.7 = (bf16[1,16,256]{2,1,0:T(8,128)(2,1)S(1)}, bf16[1,16,256]{2,1,0:T(8,128)(2,1)S(1)}, u32[]{:S(2)}, u32[]{:S(2)}) collective-permute-start(bf16[1,16,256]{2,1,0:T(8,128)(2,1)S(1)} %convert_element_type.102), channel_id=1, source_target_pairs={{0,8},{1,9},{2,10},{3,11},{4,12},{5,13},{6,14},{7,15},{8,0},{9,1},... | collective-permute-start | bytes 24584 | tf_op jit(solution)/shard_map/ppermute | solution.py:24
  104.2 22.7 %collective-permute-start.8 = (bf16[1,16,256]{2,1,0:T(8,128)(2,1)S(1)}, bf16[1,16,256]{2,1,0:T(8,128)(2,1)S(1)}, u32[]{:S(2)}, u32[]{:S(2)}) collective-permute-start(bf16[1,16,256]{2,1,0:T(8,128)(2,1)S(1)} %convert_element_type.102), channel_id=1, source_target_pairs={{0,9},{1,8},{2,11},{3,10},{4,13},{5,12},{6,15},{7,14},{8,1},{9,0},... | collective-permute-start | bytes 24584 | tf_op jit(solution)/shard_map/ppermute | solution.py:24
  110.6 18.3 %collective-permute-start.9 = (bf16[1,16,256]{2,1,0:T(8,128)(2,1)S(1)}, bf16[1,16,256]{2,1,0:T(8,128)(2,1)S(1)}, u32[]{:S(2)}, u32[]{:S(2)}) collective-permute-start(bf16[1,16,256]{2,1,0:T(8,128)(2,1)S(1)} %convert_element_type.102), channel_id=1, source_target_pairs={{0,10},{1,11},{2,8},{3,9},{4,14},{5,15},{6,12},{7,13},{8,2},{9,3},... | collective-permute-start | bytes 24584 | tf_op jit(solution)/shard_map/ppermute | solution.py:24
  112.5 21.6 %collective-permute-start.10 = (bf16[1,16,256]{2,1,0:T(8,128)(2,1)S(1)}, bf16[1,16,256]{2,1,0:T(8,128)(2,1)S(1)}, u32[]{:S(2)}, u32[]{:S(2)}) collective-permute-start(bf16[1,16,256]{2,1,0:T(8,128)(2,1)S(1)} %convert_element_type.102), channel_id=1, source_target_pairs={{0,11},{1,10},{2,9},{3,8},{4,15},{5,14},{6,13},{7,12},{8,3},{9,2},... | collective-permute-start | bytes 24584 | tf_op jit(solution)/shard_map/ppermute | solution.py:24
  119.6 14.6 %collective-permute-start.11 = (bf16[1,16,256]{2,1,0:T(8,128)(2,1)S(1)}, bf16[1,16,256]{2,1,0:T(8,128)(2,1)S(1)}, u32[]{:S(2)}, u32[]{:S(2)}) collective-permute-start(bf16[1,16,256]{2,1,0:T(8,128)(2,1)S(1)} %convert_element_type.102), channel_id=1, source_target_pairs={{0,12},{1,13},{2,14},{3,15},{4,8},{5,9},{6,10},{7,11},{8,4},{9,5},... | collective-permute-start | bytes 24584 | tf_op jit(solution)/shard_map/ppermute | solution.py:24
  121.5 12.6 %collective-permute-start.12 = (bf16[1,16,256]{2,1,0:T(8,128)(2,1)S(1)}, bf16[1,16,256]{2,1,0:T(8,128)(2,1)S(1)}, u32[]{:S(2)}, u32[]{:S(2)}) collective-permute-start(bf16[1,16,256]{2,1,0:T(8,128)(2,1)S(1)} %convert_element_type.102), channel_id=1, source_target_pairs={{0,13},{1,12},{2,15},{3,14},{4,9},{5,8},{6,11},{7,10},{8,5},{9,4},... | collective-permute-start | bytes 24584 | tf_op jit(solution)/shard_map/ppermute | solution.py:24
  126.9 7.3 %collective-permute-start.13 = (bf16[1,16,256]{2,1,0:T(8,128)(2,1)S(1)}, bf16[1,16,256]{2,1,0:T(8,128)(2,1)S(1)}, u32[]{:S(2)}, u32[]{:S(2)}) collective-permute-start(bf16[1,16,256]{2,1,0:T(8,128)(2,1)S(1)} %convert_element_type.102), channel_id=1, source_target_pairs={{0,14},{1,15},{2,12},{3,13},{4,10},{5,11},{6,8},{7,9},{8,6},{9,7},... | collective-permute-start | bytes 24584 | tf_op jit(solution)/shard_map/ppermute | solution.py:24
  128.9 6.6 %collective-permute-start.14 = (bf16[1,16,256]{2,1,0:T(8,128)(2,1)S(1)}, bf16[1,16,256]{2,1,0:T(8,128)(2,1)S(1)}, u32[]{:S(2)}, u32[]{:S(2)}) collective-permute-start(bf16[1,16,256]{2,1,0:T(8,128)(2,1)S(1)} %convert_element_type.102), channel_id=1, source_target_pairs={{0,15},{1,14},{2,13},{3,12},{4,11},{5,10},{6,9},{7,8},{8,7},{9,6},... | collective-permute-start | bytes 24584 | tf_op jit(solution)/shard_map/ppermute | solution.py:24
  136.0 7.3 %copy-start.3 = (bf16[16,64,128]{2,1,0:T(8,128)(2,1)S(1)}, bf16[16,64,128]{2,1,0:T(8,128)(2,1)}, u32[]{:S(2)}) copy-start(bf16[16,64,128]{2,1,0:T(8,128)(2,1)} %param.9) | copy-start | bytes 786436
Sparse Core Ops, SparseCore 0:
  9.5 65.3 all-gather.1
